TPU v7x, 512 devices: a whole 4x4x16 slice. The times are simulated.
512 devices in a mesh: ax: 32 (over z, x_hi), pen: 16 (over x_lo, y, core).
Axes of the slice: x: 4 (x_hi: 2, x_lo: 2; x = x_hi * 2 + x_lo), y: 4, z: 16, core: 2. Of those that a mesh axis runs over, the one named last changes fastest.
Arguments:
- fields: float32 [2, 5, 512, 192, 128], P(None, None, 'ax', 'pen'), may hold values from -0.8 to 0.8, as said below
- axial_mean: float32 [512, 192, 128], P('ax', 'pen'), may hold values from 0.2 to 1.5
- radial_mean: float32 [512, 192, 128], P('ax', 'pen'), may hold values from -0.3 to 0.3
- swirl_mean: float32 [512, 192, 128], P('ax', 'pen'), may hold values from -0.3 to 0.3
- density: float32 [512, 192, 128], P('ax', 'pen'), may hold values from 0.5 to 2
- pressure: float32 [512, 192, 128], P('ax', 'pen'), may hold values from 0.4 to 1.2
Outputs:
- residual: float32 [2, 5, 512, 192, 128], P(None, None, 'ax', 'pen')
Inputs may be any that keep to these rules, and one draw needn't show every extreme that they name: `fields`: each entry is a draw times (1 - c_j^2)^2 with c_j = cos(pi j / 191) at radial node j, so every field vanishes at both radial ends.
All inputs are finite; a program needn't handle non-finite values.
Results may differ from a plain program's by a relative error of at most 0.0001.
Values sent between devices are 32-bit elements; how exact they have to be, the bound alone decides.
No kernel may reach another device: no remote copies, remote signals or barrier semaphores. Data moves between devices by JAX's collectives and lax.ppermute only.
A program may use at most 64 MiB of HBM per device.

v0:
```python
import jax
import jax.numpy as jnp
import numpy as np
from jax import lax
from jax.sharding import PartitionSpec as P

angular_frequency = 1.7
viscosity = 0.01
conduction = 0.014
gamma_ratio = 1.4
spacing = 0.1
radius_inner = 0.5
radius_outer = 6.5
first_axial = (0.8, -0.2, 4.0 / 105.0, -1.0 / 280.0)
axial_second_derivative = (-205.0 / 72.0, 1.6, -0.2, 8.0 / 315.0, -1.0 / 560.0)
highest = lax.Precision.HIGHEST


def with_halo(array, sides, width):
    for axis, dim in sides:
        size, length = (lax.axis_size(axis), array.shape[dim])
        up = [(i, (i + 1) % size) for i in range(size - 1)]
        down = [(j, i) for i, j in up]
        last = lax.slice_in_dim(array, length - width, length, axis=dim)
        initial = lax.slice_in_dim(array, 0, width, axis=dim)
        before = lax.ppermute(last, axis, up)
        after = lax.ppermute(initial, axis, down)
        array = jnp.concatenate([before, array, after], axis=dim)
    return array


def cheb_tables(node_count):
    last_node = node_count - 1
    node_index = np.arange(node_count)
    cheb_nodes = np.cos(np.pi * node_index / last_node)
    end_weight = np.where((node_index == 0) | (node_index == last_node), 2.0, 1.0) * np.where(
        node_index % 2 == 0, 1.0, -1.0
    )
    row_index = node_index[:, None]
    col_index = node_index[None, :]
    node_gap = (
        -2.0
        * np.sin(np.pi * (row_index + col_index) / (2 * last_node))
        * np.sin(np.pi * (row_index - col_index) / (2 * last_node))
    )
    off_diag = row_index != col_index
    safe_gap = np.where(off_diag, node_gap, 1.0)
    matrix = np.where(off_diag, end_weight[:, None] / end_weight[None, :] / safe_gap, 0.0)
    row_total = matrix.sum(axis=1)
    matrix = np.where(off_diag, matrix, -row_total[:, None])
    order_first_terms = matrix * (-2.0 / (radius_outer - radius_inner))
    second_order = order_first_terms @ order_first_terms
    radius_nodes = radius_inner + (radius_outer - radius_inner) * (1.0 - cheb_nodes) / 2.0
    return (order_first_terms, second_order, radius_nodes)


def fourier_tables(point_count):
    offsets = np.arange(point_count)[:, None] - np.arange(point_count)[None, :]
    half_angle = np.pi * offsets / point_count
    sign_table = np.where(offsets % 2 == 0, 1.0, -1.0)
    nonzero = offsets != 0
    safe_sine = np.where(nonzero, np.sin(half_angle), 1.0)
    order_first_terms = np.where(nonzero, 0.5 * sign_table * np.cos(half_angle) / safe_sine, 0.0)
    second_order = np.where(
        nonzero, -0.5 * sign_table / safe_sine**2, -(point_count**2) / 12.0 - 1.0 / 6.0
    )
    return (order_first_terms, second_order)


def build_work(fields, density, pressure):
    thermal_field = fields[:, 4] / density - pressure * fields[:, 3] / (density * density)
    return jnp.concatenate([fields[:, :3], thermal_field[:, None], fields[:, 3:]], axis=1)


def axial_derivatives(padded, planes):

    def shifted(source, offset):
        return lax.slice_in_dim(source, 4 + offset, 4 + offset + planes, axis=2)

    lower = padded[:, :4]
    slope_x = first_axial[0] * (shifted(padded, 1) - shifted(padded, -1))
    curve_x = axial_second_derivative[0] * shifted(lower, 0)
    for offset in range(1, 5):
        if offset > 1:
            slope_x = slope_x + first_axial[offset - 1] * (
                shifted(padded, offset) - shifted(padded, -offset)
            )
        curve_x = curve_x + axial_second_derivative[offset] * (
            shifted(lower, offset) + shifted(lower, -offset)
        )
    return (slope_x / spacing, curve_x / (spacing * spacing))


def theta_derivatives(work_fields, theta_first, azimuthal_second_derivative):
    slope_t = jnp.dot(work_fields, theta_first, precision=highest)
    curve_t = jnp.dot(work_fields[:, :4], azimuthal_second_derivative, precision=highest)
    return (slope_t, curve_t)


def radial_derivatives(pencil_block, radial_first, radial_second):
    slope_r = jnp.einsum("sj,abxjt->abxst", radial_first, pencil_block, precision=highest)
    curve_r = jnp.einsum("sj,abxjt->abxst", radial_second, pencil_block[:, :4], precision=highest)
    return (slope_r, curve_r)


def rotate_phase(value):
    return jnp.stack([-angular_frequency * value[1], angular_frequency * value[0]])


def radial_terms(slope_r, curve_r, radial_mean, density, pressure, inv_radius):
    laplace = curve_r + slope_r[:, :4] * inv_radius
    convect = radial_mean * slope_r
    term_u = convect[:, 0] - viscosity * laplace[:, 0]
    term_v = convect[:, 1] + slope_r[:, 5] / density - viscosity * laplace[:, 1]
    term_w = convect[:, 2] - viscosity * laplace[:, 2]
    term_rho = convect[:, 4] + density * slope_r[:, 1]
    term_p = convect[:, 5] + gamma_ratio * pressure * slope_r[:, 1] - conduction * laplace[:, 3]
    return jnp.stack([term_u, term_v, term_w, term_rho, term_p], axis=1)


def other_terms(
    work_fields,
    slope_x,
    curve_x,
    slope_t,
    curve_t,
    axial_mean,
    radial_mean,
    swirl_mean,
    density,
    pressure,
    inv_radius,
):
    inv_square = inv_radius * inv_radius
    convect = axial_mean * slope_x + swirl_mean * inv_radius * slope_t
    laplace = curve_x + inv_square * curve_t
    vel_u = work_fields[:, 0]
    vel_v = work_fields[:, 1]
    vel_w = work_fields[:, 2]
    div_part = slope_x[:, 0] + inv_radius * (vel_v + slope_t[:, 2])
    term_u = (
        rotate_phase(vel_u) + convect[:, 0] + slope_x[:, 5] / density - viscosity * laplace[:, 0]
    )
    term_v = (
        rotate_phase(vel_v)
        + convect[:, 1]
        - 2.0 * swirl_mean * inv_radius * vel_w
        - viscosity * (laplace[:, 1] - inv_square * (vel_v + 2.0 * slope_t[:, 2]))
    )
    term_w = (
        rotate_phase(vel_w)
        + convect[:, 2]
        + inv_radius * slope_t[:, 5] / density
        + inv_radius * (radial_mean * vel_w + swirl_mean * vel_v)
        - viscosity * (laplace[:, 2] - inv_square * (vel_w - 2.0 * slope_t[:, 1]))
    )
    term_rho = rotate_phase(work_fields[:, 4]) + convect[:, 4] + density * div_part
    term_p = (
        rotate_phase(work_fields[:, 5])
        + convect[:, 5]
        + gamma_ratio * pressure * div_part
        - conduction * laplace[:, 3]
    )
    return jnp.stack([term_u, term_v, term_w, term_rho, term_p], axis=1)


def per_device(fields, axial_mean, radial_mean, swirl_mean, density, pressure):
    planes = fields.shape[2]
    shard_rows = fields.shape[3]
    grid_points = fields.shape[4]
    total_rows = shard_rows * lax.axis_size("pen")
    first_np, second_np, radius_np = cheb_tables(total_rows)
    radial_first = jnp.asarray(first_np, jnp.float32)
    radial_second = jnp.asarray(second_np, jnp.float32)
    inv_all = jnp.asarray(1.0 / radius_np, jnp.float32)[:, None]
    inv_local = lax.dynamic_slice_in_dim(inv_all, lax.axis_index("pen") * shard_rows, shard_rows, 0)
    theta_np, theta_second_np = fourier_tables(grid_points)
    theta_first = jnp.asarray(theta_np.T, jnp.float32)
    azimuthal_second_derivative = jnp.asarray(theta_second_np.T, jnp.float32)
    work_fields = build_work(fields, density, pressure)
    padded = with_halo(work_fields, (("ax", 2),), 4)
    slope_x, curve_x = axial_derivatives(padded, planes)
    slope_t, curve_t = theta_derivatives(work_fields, theta_first, azimuthal_second_derivative)
    slope_r, curve_r = radial_derivatives(
        lax.all_to_all(work_fields, "pen", split_axis=2, concat_axis=3, tiled=True),
        radial_first,
        radial_second,
    )
    slope_r, curve_r = (
        lax.all_to_all(slope_r, "pen", split_axis=3, concat_axis=2, tiled=True),
        lax.all_to_all(curve_r, "pen", split_axis=3, concat_axis=2, tiled=True),
    )
    radial_component = radial_terms(slope_r, curve_r, radial_mean, density, pressure, inv_local)
    return radial_component + other_terms(
        work_fields,
        slope_x,
        curve_x,
        slope_t,
        curve_t,
        axial_mean,
        radial_mean,
        swirl_mean,
        density,
        pressure,
        inv_local,
    )


def solution(mesh):
    placed = (
        P(None, None, "ax", "pen", None),
        P("ax", "pen", None),
        P("ax", "pen", None),
        P("ax", "pen", None),
        P("ax", "pen", None),
        P("ax", "pen", None),
    )
    return jax.shard_map(
        per_device,
        mesh=mesh,
        in_specs=placed,
        out_specs=P(None, None, "ax", "pen", None),
        check_vma=False,
    )
```

profile of v0, /device:TPU:4, one launch (start us, length us, event | category | flops | bytes accessed | tf_op | source)
XLA Modules:
  0.0 97.6 jit_solution(14125094061628838863)
XLA Ops:
  0.0 1.2 %slice.244 = f32[2,3,16,12,128]{4,2,3,1,0:T(8,128)S(1)} slice(f32[2,5,16,12,128]{4,2,3,1,0:T(8,128)} %param.11), slice={[0:2], [0:3], [0:16], [0:12], [0:128]} | slice | bytes 1179648 | tf_op jit(solution)/shard_map/slice | solution.py:72
  1.2 0.2 copy-done
  1.4 0.0 copy-done.1
  1.4 0.0 copy-done.18
  1.5 0.1 divide_subtract_fusion
  1.5 0.1 pad_maximum_fusion.1
  1.6 2.0 %copy.44 = f32[2,6,16,12,128]{4,0,3,1,2:T(2,128)} copy(f32[2,6,16,12,128]{4,2,3,1,0:T(8,128)S(1)} %pad_maximum_fusion.1) | data formatting | bytes 2359296 | tf_op jit(solution)/shard_map/concatenate | solution.py:72
  3.6 5.3 %all-to-all-start = ((f32[2,6,16,12,128]{4,0,3,1,2:T(2,128)}), f32[2,6,16,12,128]{4,0,3,1,2:T(2,128)}, u32[]{:S(2)}, u32[]{:S(2)}) async-start(f32[2,6,16,12,128]{4,0,3,1,2:T(2,128)} %copy.44), calls=%async_computation | async-start | bytes 2359296 | tf_op jit(solution)/shard_map/all_to_all | solution.py:185
  8.8 0.0 copy-start.25
  8.8 0.0 copy-start.8
  8.9 0.9 fusion.53
  9.8 6.9 %collective-permute-start = (f32[2,6,4,12,128]{4,2,3,1,0:T(4,128)}, f32[2,6,4,12,128]{4,2,3,1,0:T(4,128)S(1)}, u32[]{:S(2)}, u32[]{:S(2)}) collective-permute-start(f32[2,6,4,12,128]{4,2,3,1,0:T(4,128)} %get-tuple-element.11), channel_id=1, source_target_pairs={{16,0},{32,16},{48,32},{64,48},{80,64},{96,80},{112,96},{128,112},... | collective-permute-start | bytes 884744 | tf_op jit(solution)/shard_map/ppermute | solution.py:27
  16.7 1.9 %collective-permute-start.1 = (f32[2,6,4,12,128]{4,2,3,1,0:T(4,128)}, f32[2,6,4,12,128]{4,2,3,1,0:T(4,128)S(1)}, u32[]{:S(2)}, u32[]{:S(2)}) collective-permute-start(f32[2,6,4,12,128]{4,2,3,1,0:T(4,128)} %get-tuple-element.12), channel_id=1, source_target_pairs={{0,16},{16,32},{32,48},{48,64},{64,80},{80,96},{96,112},{112,128},... | collective-permute-start | bytes 884744 | tf_op jit(solution)/shard_map/ppermute | solution.py:26
  18.6 0.0 copy-done.25
  18.6 0.1 broadcast_multiply_fusion.6
  18.7 0.0 copy-done.8
  18.7 1.7 %broadcast_multiply_fusion.2 = (f32[16,12,128]{2,0,1:T(8,128)}, f32[16,12,128]{2,0,1:T(8,128)}, f32[16,12,128]{2,0,1:T(8,128)}) fusion(f32[16,12,128]{2,0,1:T(8,128)S(1)} %copy-done.8, f32[12]{0:T(128)S(1)} %get-tuple-element.30, f32[12]{0:T(128)S(1)} %get-tuple-element.32, f32[16,12,128]{2,0,1:T(8,128)} %param.12), kind=kLoop, calls=%fused_computation.100 | loop fusion | flops 73728 | bytes 491616 | tf_op jit(solution)/shard_map/mul | solution.py:147
  20.4 0.9 broadcast_multiply_fusion.5
  21.3 1.0 slice_multiply_fusion.10
  22.3 6.7 %collective-permute-done = f32[2,6,4,12,128]{4,2,3,1,0:T(4,128)S(1)} collective-permute-done((f32[2,6,4,12,128]{4,2,3,1,0:T(4,128)}, f32[2,6,4,12,128]{4,2,3,1,0:T(4,128)S(1)}, u32[]{:S(2)}, u32[]{:S(2)}) %collective-permute-start) | collective-permute-done | bytes 294944 | tf_op jit(solution)/shard_map/ppermute | solution.py:27
  28.9 11.4 %collective-permute-done.1 = f32[2,6,4,12,128]{4,2,3,1,0:T(4,128)S(1)} collective-permute-done((f32[2,6,4,12,128]{4,2,3,1,0:T(4,128)}, f32[2,6,4,12,128]{4,2,3,1,0:T(4,128)S(1)}, u32[]{:S(2)}, u32[]{:S(2)}) %collective-permute-start.1) | collective-permute-done | bytes 294944 | tf_op jit(solution)/shard_map/ppermute | solution.py:26
  40.4 2.1 %pad_maximum_fusion = (f32[2,6,20,12,128]{4,2,3,1,0:T(8,128)}, f32[2,6,20,12,128]{4,2,3,1,0:T(8,128)}) fusion(f32[2,6,4,12,128]{4,2,3,1,0:T(4,128)S(1)} %collective-permute-done, f32[2,2,16,12,128]{4,2,3,1,0:T(8,128)S(1)} %slice.247, f32[2,1,16,12,128]{4,2,3,1,0:T(8,128)S(1)} %divide_subtract_fusion, f32[2,3,16,12,128]{4,2,3,1,0:T(8,128)S(1)} %slice.244, ...), kind=kLoop, calls=%fused_computation | loop fusion | flops 2211840 | bytes 4718592 | tf_op jit(solution)/shard_map/concatenate | solution.py:28
  42.5 0.0 all-to-all-done
  42.5 1.4 %copy.45 = f32[2,6,16,12,128]{4,0,3,2,1:T(2,128)S(1)} copy(f32[2,6,16,12,128]{4,0,3,1,2:T(2,128)} %all-to-all-done) | data formatting | bytes 2359296 | tf_op jit(solution)/shard_map/all_to_all | solution.py:185
  43.9 0.0 copy-done.24
  43.9 1.2 %convolution_bitcast_fusion = f32[2,6,1,192,128]{4,3,1,0,2:T(8,128)S(1)} fusion(f32[192,192,1,1]{1,0,3,2:T(8,128)S(1)} %copy-done.24, f32[2,6,192,128]{3,0,2,1:T(2,128)S(1)} %bitcast.35), kind=kOutput, calls=%fused_computation.2 | convolution fusion | flops 679477248 | bytes 2506752 | tf_op jit(solution)/shard_map/sj,abxjt->abxst/dot_general | solution.py:101
  45.1 1.9 %copy.47 = f32[2,6,1,192,128]{4,0,2,1,3:T(2,128)} copy(f32[2,6,1,192,128]{4,3,1,0,2:T(8,128)S(1)} %convolution_bitcast_fusion) | data formatting | bytes 2359296 | tf_op jit(solution)/shard_map/sj,abxjt->abxst/transpose | solution.py:101
  47.1 6.2 %all-to-all-start.1 = ((f32[2,6,1,192,128]{4,0,2,1,3:T(2,128)}), f32[2,6,1,192,128]{4,0,2,1,3:T(2,128)}, u32[]{:S(2)}, u32[]{:S(2)}) async-start(f32[2,6,1,192,128]{4,0,2,1,3:T(2,128)} %copy.47), calls=%async_computation.1 | async-start | bytes 2359296 | tf_op jit(solution)/shard_map/all_to_all | solution.py:190
  53.3 8.7 %multiply_add_fusion = (f32[2,6,16,12,128]{4,2,3,1,0:T(8,128)S(1)}, f32[2,6,16,12,128]{4,2,3,1,0:T(8,128)S(1)}, f32[2,6,16,12,128]{4,2,3,1,0:T(8,128)}) fusion(f32[16,12,128]{2,0,1:T(8,128)} %get-tuple-element.29, f32[16,12,128]{2,0,1:T(8,128)} %get-tuple-element.34, f32[2,6,20,12,128]{4,2,3,1,0:T(8,128)} %get-tuple-element.10, ...), kind=kOutput, calls=%fused_computation.19 | convolution fusion | flops 457703424 | bytes 14417920 | tf_op jit(solution)/shard_map/dot_general | solution.py:95
  62.0 0.1 broadcast_multiply_fusion
  62.1 0.0 copy-start.2
  62.1 0.8 copy-done.26
  62.9 5.3 %fusion = f32[2,4,16,12,128]{4,2,3,1,0:T(8,128)S(1)} fusion(f32[128,128,1,1,1]{1,0,4,3,2:T(8,128)S(1)} %copy-done.26, f32[2,6,20,12,128]{4,2,3,1,0:T(8,128)} %get-tuple-element.10, f32[2,6,20,12,128]{4,2,3,1,0:T(8,128)} %get-tuple-element.9, f32[2,1,16,12,128]{4,2,3,1,0:T(8,128)S(1)} %divide_subtract_fusion, f32[2,3,16,12,128]{4,2,3,1,0:T(8,128)S(1)} %slice.244, ...), kind=kOutput, calls=%fused_computation.5 | convolution fusion | flops 305528832 | bytes 8716800 | tf_op jit(solution)/shard_map/dot_general | solution.py:96
  68.2 0.0 copy-start.6
  68.2 0.0 copy-done.5
  68.2 0.0 copy-done.2
  68.3 0.0 copy-done.19
  68.3 0.0 copy-done.20
  68.3 0.0 copy-start.23
  68.3 0.1 fusion.38
  68.4 0.1 slice.306
  68.4 0.7 copy-done.6
  69.1 0.3 copy-done.23
  69.4 0.9 convolution_bitcast_fusion.1
  70.3 1.4 %copy.52 = f32[2,4,1,192,128]{4,1,0,2,3:T(4,128)} copy(f32[2,4,1,192,128]{4,3,1,0,2:T(8,128)S(1)} %convolution_bitcast_fusion.1) | data formatting | bytes 1572864 | tf_op jit(solution)/shard_map/sj,abxjt->abxst/transpose | solution.py:102
  71.7 0.0 copy-start.10
  71.7 0.0 copy-start.16
  71.7 0.0 copy-start.17
  71.7 0.0 all-to-all-done.1
  71.7 5.9 %all-to-all-start.2 = ((f32[2,4,1,192,128]{4,1,0,2,3:T(4,128)}), f32[2,4,1,192,128]{4,1,0,2,3:T(4,128)}, u32[]{:S(2)}, u32[]{:S(2)}) async-start(f32[2,4,1,192,128]{4,1,0,2,3:T(4,128)} %copy.52), calls=%async_computation.2 | async-start | bytes 1572864 | tf_op jit(solution)/shard_map/all_to_all | solution.py:191
  77.6 1.2 %fusion.35 = f32[2,5,16,12,128]{4,2,3,1,0:T(8,128)S(1)} fusion(f32[2,5,16,12,128]{4,2,3,1,0:T(8,128)S(1)} %fusion.38, f32[2,4,16,12,128]{4,2,3,1,0:T(8,128)S(1)} %copy-done.7, f32[2,6,16,12,128]{4,2,3,1,0:T(8,128)} %copy-done.5, f32[1,1,16,12,128]{4,2,3,1,0:T(8,128)S(1)} %copy-done.22, f32[1,1,16,12,128]{4,2,3,1,0:T(8,128)} %get-tuple-element.20, ...), kind=kLoop, calls=%fused_computation.63 | loop fusion | flops 491520 | bytes 1475072
  78.8 0.0 copy-start.11
  78.9 1.3 %fusion.29 = f32[2,5,16,12,128]{4,2,3,1,0:T(8,128)S(1)} fusion(f32[2,5,16,12,128]{4,2,3,1,0:T(8,128)S(1)} %fusion.35, f32[2,6,16,12,128]{4,2,3,1,0:T(8,128)} %get-tuple-element.33, f32[2,4,16,12,128]{4,2,3,1,0:T(8,128)S(1)} %copy-done.7, f32[2,6,16,12,128]{4,2,3,1,0:T(8,128)} %copy-done.5, f32[1,1,16,12,128]{4,2,3,1,0:T(8,128)S(1)} %copy-done.16, ...), kind=kLoop, calls=%fused_computation.54 | loop fusion | flops 786432 | bytes 1868800
  80.1 0.0 copy-start.3
  80.1 0.9 copy-done.3
  81.1 0.0 copy-done.11
  81.1 1.7 %broadcast_multiply_fusion.1 = (f32[2,6,16,12,128]{4,2,3,1,0:T(8,128)S(1)}, f32[2,6,16,12,128]{4,2,3,1,0:T(8,128)S(1)}) fusion(f32[16,12,128]{2,0,1:T(8,128)S(1)} %copy-done.11, f32[2,6,16,12,128]{4,0,1,3,2:T(2,128)} %bitcast.6), kind=kLoop, calls=%fused_computation.38 | loop fusion | flops 294912 | bytes 3637248 | tf_op jit(solution)/shard_map/mul | solution.py:112
  82.7 8.6 %all-to-all-done.2 = f32[2,4,1,192,128]{4,1,0,2,3:T(4,128)} async-done(((f32[2,4,1,192,128]{4,1,0,2,3:T(4,128)}), f32[2,4,1,192,128]{4,1,0,2,3:T(4,128)}, u32[]{:S(2)}, u32[]{:S(2)}) %all-to-all-start.2) | async-done | bytes 786464 | tf_op jit(solution)/shard_map/all_to_all | solution.py:191
  91.4 1.7 %fusion.18 = f32[2,4,16,12,128]{4,2,3,1,0:T(8,128)S(1)} fusion(f32[2,6,16,12,128]{4,2,3,1,0:T(8,128)S(1)} %get-tuple-element.14, f32[2,4,16,12,128]{4,1,0,3,2:T(4,128)} %bitcast.13, f32[12]{0:T(128)S(1)} %get-tuple-element.32), kind=kLoop, calls=%fused_computation.34 | loop fusion | flops 393216 | bytes 2359344 | tf_op jit(solution)/shard_map/add | solution.py:111
  93.2 1.2 %fusion.23 = (f32[2,5,16,12,128]{4,2,3,1,0:T(8,128)S(1)}, f32[2,1,16,12,128]{4,2,3,1,0:T(8,128)S(1)}, f32[2,5,16,12,128]{4,2,3,1,0:T(8,128)S(1)}) fusion(f32[2,5,16,12,128]{4,2,3,1,0:T(8,128)S(1)} %copy-done.4, f32[2,6,16,12,128]{4,2,3,1,0:T(8,128)} %copy-done.5, f32[1,1,16,12,128]{4,2,3,1,0:T(8,128)S(1)} %copy-done.15, ...), kind=kLoop, calls=%fused_computation.47 | loop fusion | flops 540672 | bytes 2261504
  94.5 0.8 copy-done.12
  95.3 0.0 copy-done.13
  95.3 1.1 %fusion.20 = (f32[2,5,16,12,128]{4,2,3,1,0:T(8,128)S(1)}, f32[2,5,16,12,128]{4,2,3,1,0:T(8,128)S(1)}) fusion(f32[2,5,16,12,128]{4,2,3,1,0:T(8,128)S(1)} %get-tuple-element.5, f32[2,4,16,12,128]{4,2,3,1,0:T(8,128)} %copy-done.6, f32[2,6,16,12,128]{4,2,3,1,0:T(8,128)} %copy-done.5, f32[1,1,16,12,128]{4,2,3,1,0:T(8,128)S(1)} %copy-done.13, ...), kind=kLoop, calls=%fused_computation.41 | loop fusion | flops 491520 | bytes 1867776 | tf_op jit(solution)/shard_map/stack | solution.py:164
  96.5 1.1 %add.150 = f32[2,5,16,12,128]{4,2,3,1,0:T(8,128)} add(f32[2,5,16,12,128]{4,2,3,1,0:T(8,128)S(1)} %get-tuple-element.26, f32[2,5,16,12,128]{4,2,3,1,0:T(8,128)S(1)} %get-tuple-element.25) | non-fusion elementwise | flops 245760 | bytes 2949120 | tf_op jit(solution)/shard_map/add | solution.py:194
  (32 shorter events, 0.2 us)
Async XLA Ops:
  0.0 1.4 %copy-start = (f32[2,5,16,12,128]{4,2,3,1,0:T(8,128)S(1)}, f32[2,5,16,12,128]{4,2,3,1,0:T(8,128)}, u32[]{:S(2)}) copy-start(f32[2,5,16,12,128]{4,2,3,1,0:T(8,128)} %param.11) | copy-start | bytes 2949124
  0.0 1.4 %copy-start.1 = (f32[16,12,128]{2,0,1:T(8,128)S(1)}, f32[16,12,128]{2,0,1:T(8,128)}, u32[]{:S(2)}) copy-start(f32[16,12,128]{2,0,1:T(8,128)} %param.15) | copy-start | bytes 294916
  0.0 1.4 %copy-start.18 = (f32[16,12,128]{2,0,1:T(8,128)S(1)}, f32[16,12,128]{2,0,1:T(8,128)}, u32[]{:S(2)}) copy-start(f32[16,12,128]{2,0,1:T(8,128)} %param.16) | copy-start | bytes 294916
  3.6 38.9 %all-to-all-start = ((f32[2,6,16,12,128]{4,0,3,1,2:T(2,128)}), f32[2,6,16,12,128]{4,0,3,1,2:T(2,128)}, u32[]{:S(2)}, u32[]{:S(2)}) async-start(f32[2,6,16,12,128]{4,0,3,1,2:T(2,128)} %copy.44), calls=%async_computation | async-start | bytes 2359296 | tf_op jit(solution)/shard_map/all_to_all | solution.py:185
  8.8 9.8 %copy-start.25 = (f32[192]{0:T(256)S(1)}, f32[192]{0:T(256)}, u32[]{:S(2)}) copy-start(f32[192]{0:T(256)} %constant.58.clone) | copy-start | bytes 2308
  8.8 9.8 %copy-start.8 = (f32[16,12,128]{2,0,1:T(8,128)S(1)}, f32[16,12,128]{2,0,1:T(8,128)}, u32[]{:S(2)}) copy-start(f32[16,12,128]{2,0,1:T(8,128)} %param.14) | copy-start | bytes 294916
  9.8 19.2 %collective-permute-start = (f32[2,6,4,12,128]{4,2,3,1,0:T(4,128)}, f32[2,6,4,12,128]{4,2,3,1,0:T(4,128)S(1)}, u32[]{:S(2)}, u32[]{:S(2)}) collective-permute-start(f32[2,6,4,12,128]{4,2,3,1,0:T(4,128)} %get-tuple-element.11), channel_id=1, source_target_pairs={{16,0},{32,16},{48,32},{64,48},{80,64},{96,80},{112,96},{128,112},... | collective-permute-start | bytes 884744 | tf_op jit(solution)/shard_map/ppermute | solution.py:27
  16.7 23.7 %collective-permute-start.1 = (f32[2,6,4,12,128]{4,2,3,1,0:T(4,128)}, f32[2,6,4,12,128]{4,2,3,1,0:T(4,128)S(1)}, u32[]{:S(2)}, u32[]{:S(2)}) collective-permute-start(f32[2,6,4,12,128]{4,2,3,1,0:T(4,128)} %get-tuple-element.12), channel_id=1, source_target_pairs={{0,16},{16,32},{32,48},{48,64},{64,80},{80,96},{96,112},{112,128},... | collective-permute-start | bytes 884744 | tf_op jit(solution)/shard_map/ppermute | solution.py:26
  42.5 1.4 %copy-start.24 = (f32[192,192,1,1]{1,0,3,2:T(8,128)S(1)}, f32[192,192,1,1]{1,0,3,2:T(8,128)}, u32[]{:S(2)}) copy-start(f32[192,192,1,1]{1,0,3,2:T(8,128)} %constant.67) | copy-start | bytes 442372
  47.1 24.6 %all-to-all-start.1 = ((f32[2,6,1,192,128]{4,0,2,1,3:T(2,128)}), f32[2,6,1,192,128]{4,0,2,1,3:T(2,128)}, u32[]{:S(2)}, u32[]{:S(2)}) async-start(f32[2,6,1,192,128]{4,0,2,1,3:T(2,128)} %copy.47), calls=%async_computation.1 | async-start | bytes 2359296 | tf_op jit(solution)/shard_map/all_to_all | solution.py:190
  62.0 6.2 %copy-start.5 = (f32[2,6,16,12,128]{4,2,3,1,0:T(8,128)}, f32[2,6,16,12,128]{4,2,3,1,0:T(8,128)S(1)}, u32[]{:S(2)}) copy-start(f32[2,6,16,12,128]{4,2,3,1,0:T(8,128)S(1)} %get-tuple-element.7) | copy-start | bytes 3538948
  62.0 0.9 copy-start.26
  62.1 6.1 %copy-start.2 = (f32[2,6,16,12,128]{4,2,3,1,0:T(8,128)}, f32[2,6,16,12,128]{4,2,3,1,0:T(8,128)S(1)}, u32[]{:S(2)}) copy-start(f32[2,6,16,12,128]{4,2,3,1,0:T(8,128)S(1)} %broadcast_multiply_fusion) | copy-start | bytes 3538948
  62.9 5.4 %copy-start.19 = (f32[1,1,16,12,128]{4,2,3,1,0:T(8,128)S(1)}, f32[1,1,16,12,128]{4,2,3,1,0:T(8,128)}, u32[]{:S(2)}) copy-start(f32[1,1,16,12,128]{4,2,3,1,0:T(8,128)} %get-tuple-element.21) | copy-start | bytes 294916
  62.9 5.4 %copy-start.20 = (f32[1,1,16,12,128]{4,2,3,1,0:T(8,128)S(1)}, f32[1,1,16,12,128]{4,2,3,1,0:T(8,128)}, u32[]{:S(2)}) copy-start(f32[1,1,16,12,128]{4,2,3,1,0:T(8,128)} %get-tuple-element.22) | copy-start | bytes 294916
  68.2 0.9 copy-start.6
  68.3 1.2 %copy-start.23 = (f32[192,192,1,1]{1,0,3,2:T(8,128)S(1)}, f32[192,192,1,1]{1,0,3,2:T(8,128)}, u32[]{:S(2)}) copy-start(f32[192,192,1,1]{1,0,3,2:T(8,128)} %constant.68) | copy-start | bytes 442372
  71.7 5.9 %copy-start.7 = (f32[2,4,16,12,128]{4,2,3,1,0:T(8,128)S(1)}, f32[2,4,16,12,128]{4,2,3,1,0:T(8,128)}, u32[]{:S(2)}) copy-start(f32[2,4,16,12,128]{4,2,3,1,0:T(8,128)} %copy-done.6) | copy-start | bytes 2359300
  71.7 5.9 %copy-start.21 = (f32[16,12,128]{2,0,1:T(8,128)S(1)}, f32[16,12,128]{2,0,1:T(8,128)}, u32[]{:S(2)}) copy-start(f32[16,12,128]{2,0,1:T(8,128)} %get-tuple-element.28) | copy-start | bytes 294916
  71.7 5.9 %copy-start.22 = (f32[1,1,16,12,128]{4,2,3,1,0:T(8,128)S(1)}, f32[1,1,16,12,128]{4,2,3,1,0:T(8,128)}, u32[]{:S(2)}) copy-start(f32[1,1,16,12,128]{4,2,3,1,0:T(8,128)} %get-tuple-element.19) | copy-start | bytes 294916
  71.7 7.1 %copy-start.9 = (f32[16,12,128]{2,0,1:T(8,128)S(1)}, f32[16,12,128]{2,0,1:T(8,128)}, u32[]{:S(2)}) copy-start(f32[16,12,128]{2,0,1:T(8,128)} %param.14) | copy-start | bytes 294916
  71.7 7.1 %copy-start.10 = (f32[16,12,128]{2,0,1:T(8,128)S(1)}, f32[16,12,128]{2,0,1:T(8,128)}, u32[]{:S(2)}) copy-start(f32[16,12,128]{2,0,1:T(8,128)} %param.13) | copy-start | bytes 294916
  71.7 7.1 %copy-start.16 = (f32[1,1,16,12,128]{4,2,3,1,0:T(8,128)S(1)}, f32[1,1,16,12,128]{4,2,3,1,0:T(8,128)}, u32[]{:S(2)}) copy-start(f32[1,1,16,12,128]{4,2,3,1,0:T(8,128)} %get-tuple-element.17) | copy-start | bytes 294916
  71.7 7.1 %copy-start.17 = (f32[1,1,16,12,128]{4,2,3,1,0:T(8,128)S(1)}, f32[1,1,16,12,128]{4,2,3,1,0:T(8,128)}, u32[]{:S(2)}) copy-start(f32[1,1,16,12,128]{4,2,3,1,0:T(8,128)} %get-tuple-element.18) | copy-start | bytes 294916
  71.7 19.6 %all-to-all-start.2 = ((f32[2,4,1,192,128]{4,1,0,2,3:T(4,128)}), f32[2,4,1,192,128]{4,1,0,2,3:T(4,128)}, u32[]{:S(2)}, u32[]{:S(2)}) async-start(f32[2,4,1,192,128]{4,1,0,2,3:T(4,128)} %copy.52), calls=%async_computation.2 | async-start | bytes 1572864 | tf_op jit(solution)/shard_map/all_to_all | solution.py:191
  78.8 2.3 %copy-start.11 = (f32[16,12,128]{2,0,1:T(8,128)S(1)}, f32[16,12,128]{2,0,1:T(8,128)}, u32[]{:S(2)}) copy-start(f32[16,12,128]{2,0,1:T(8,128)} %param.13) | copy-start | bytes 294916
  80.1 0.9 copy-start.3
  91.4 1.8 %copy-start.4 = (f32[2,5,16,12,128]{4,2,3,1,0:T(8,128)S(1)}, f32[2,5,16,12,128]{4,2,3,1,0:T(8,128)}, u32[]{:S(2)}) copy-start(f32[2,5,16,12,128]{4,2,3,1,0:T(8,128)} %copy-done.3) | copy-start | bytes 2949124
  91.4 1.8 %copy-start.14 = (f32[1,1,16,12,128]{4,2,3,1,0:T(8,128)S(1)}, f32[1,1,16,12,128]{4,2,3,1,0:T(8,128)}, u32[]{:S(2)}) copy-start(f32[1,1,16,12,128]{4,2,3,1,0:T(8,128)} %get-tuple-element.16) | copy-start | bytes 294916
  91.4 1.8 %copy-start.15 = (f32[1,1,16,12,128]{4,2,3,1,0:T(8,128)S(1)}, f32[1,1,16,12,128]{4,2,3,1,0:T(8,128)}, u32[]{:S(2)}) copy-start(f32[1,1,16,12,128]{4,2,3,1,0:T(8,128)} %get-tuple-element.23) | copy-start | bytes 294916
  94.4 0.9 copy-start.12
  94.4 0.9 copy-start.13
where the time goes:
time: 98.3 us; the launch traced here: 97.6 us
  waiting for transfers between devices  26.8 us (27%)
  starting transfers between devices  26.1 us (27%)
  matrix products  16.1 us (16%)
  other arithmetic  15.4 us (16%)
  local copies, waits for them, and re-layouts  12.7 us (13%)
    ppermute x1, waiting for transfers between devices, with_halo(): before = lax.ppermute(last, axis, up)  11.4 us
    dot_general x1, matrix products, theta_derivatives(): slope_t = jnp.dot(work_fields, theta_first, precision=highest)  8.68 us
    all_to_all x1, waiting for transfers between devices, per_device(): lax.all_to_all(curve_r, 'pen', split_axis=3, concat_axis=2, tiled=True)  8.63 us
    ppermute x1, starting transfers between devices, with_halo(): after = lax.ppermute(initial, axis, down)  6.88 us
    ppermute x1, waiting for transfers between devices, with_halo(): after = lax.ppermute(initial, axis, down)  6.69 us
    all_to_all x1, starting transfers between devices, per_device(): lax.all_to_all(slope_r, 'pen', split_axis=3, concat_axis=2, tiled=True)  6.24 us
    all_to_all x1, starting transfers between devices, per_device(): lax.all_to_all(curve_r, 'pen', split_axis=3, concat_axis=2, tiled=True)  5.85 us
    dot_general x1, matrix products, theta_derivatives(): jnp.dot(work_fields[:, :4], azimuthal_second_derivative, precision=highest)  5.32 us
  transfers between devices with their start and end apart: 5, of which 3 were waited for; matrix products, arithmetic and copies ran while one was open for 28% of the time, Pallas kernels for 0%

commit v1 on v0

--- a/solution.py
+++ b/solution.py
@@ -14,6 +14,15 @@
 first_axial = (0.8, -0.2, 4.0 / 105.0, -1.0 / 280.0)
 axial_second_derivative = (-205.0 / 72.0, 1.6, -0.2, 8.0 / 315.0, -1.0 / 560.0)
 highest = lax.Precision.HIGHEST
+begin_goods_on = lambda my_tile, named_axis: jnp.concatenate(
+    lax.all_to_all(
+        jnp.stack(jnp.split(my_tile, lax.axis_size(named_axis), axis=3)),
+        axis_name=named_axis,
+        split_axis=0,
+        concat_axis=0,
+    ),
+    axis=2,
+)
 
 
 def with_halo(array, sides, width):
@@ -188,7 +197,7 @@
     )
     slope_r, curve_r = (
         lax.all_to_all(slope_r, "pen", split_axis=3, concat_axis=2, tiled=True),
-        lax.all_to_all(curve_r, "pen", split_axis=3, concat_axis=2, tiled=True),
+        begin_goods_on(curve_r, "pen"),
     )
     radial_component = radial_terms(slope_r, curve_r, radial_mean, density, pressure, inv_local)
     return radial_component + other_terms(

time: 98.3 us -> 91.5 us (0.931)
  the two profiles are of different devices: /device:TPU:4 before, /device:TPU:1 now
where the time goes in v1:
time: 91.5 us; the launch traced here: 90.7 us
  starting transfers between devices  27.9 us (30%)
  waiting for transfers between devices  26.6 us (29%)
  other arithmetic  16.6 us (18%)
  local copies, waits for them, and re-layouts  12.7 us (14%)
  matrix products  6.39 us (7%)
    all_to_all x1, waiting for transfers between devices, per_device(): lax.all_to_all(slope_r, 'pen', split_axis=3, concat_axis=2, tiled=True)  13.9 us
    all_to_all x1, starting transfers between devices, per_device(): lax.all_to_all(work_fields, 'pen', split_axis=2, concat_axis=3, tiled=True)  10.4 us
    all_to_all x1, waiting for transfers between devices, lax.all_to_all(jnp.stack(jnp.split(my_tile, lax.axis_size(named_axis), ax...  7.38 us
    ppermute x1, starting transfers between devices, with_halo(): before = lax.ppermute(last, axis, up)  6.83 us
    unnamed x7, other arithmetic  6 us
    all_to_all x1, waiting for transfers between devices, per_device(): lax.all_to_all(work_fields, 'pen', split_axis=2, concat_axis=3, tiled=True)  5.25 us
    all_to_all x1, starting transfers between devices, lax.all_to_all(jnp.stack(jnp.split(my_tile, lax.axis_size(named_axis), ax...  4.98 us
    all_to_all x1, starting transfers between devices, per_device(): lax.all_to_all(slope_r, 'pen', split_axis=3, concat_axis=2, tiled=True)  4.45 us
  transfers between devices with their start and end apart: 5, of which 3 were waited for; matrix products, arithmetic and copies ran while one was open for 22% of the time, Pallas kernels for 0%

profile of v1, /device:TPU:1, one launch (start us, length us, event | category | flops | bytes accessed | tf_op | source)
XLA Modules:
  0.0 90.7 jit_solution(7710087340681799523)
XLA Ops:
  0.0 1.1 %slice.247 = f32[2,2,16,12,128]{4,2,3,1,0:T(8,128)S(1)} slice(f32[2,5,16,12,128]{4,2,3,1,0:T(8,128)} %param.11), slice={[0:2], [3:5], [0:16], [0:12], [0:128]} | slice | bytes 786432 | tf_op jit(solution)/shard_map/slice | solution.py:81
  1.1 1.1 %slice.244 = f32[2,3,16,12,128]{4,2,3,1,0:T(8,128)S(1)} slice(f32[2,5,16,12,128]{4,2,3,1,0:T(8,128)} %param.11), slice={[0:2], [0:3], [0:16], [0:12], [0:128]} | slice | bytes 1179648 | tf_op jit(solution)/shard_map/slice | solution.py:81
  2.3 0.0 copy-done.1
  2.3 0.0 copy-done
  2.3 0.0 copy-done.18
  2.3 0.1 divide_subtract_fusion
  2.4 0.1 pad_maximum_fusion.1
  2.5 0.9 %fusion.69 = (f32[2,6,4,12,128]{4,2,3,1,0:T(4,128)}, f32[2,6,4,12,128]{4,2,3,1,0:T(4,128)}) fusion(f32[2,6,16,12,128]{4,2,3,1,0:T(8,128)S(1)} %pad_maximum_fusion.1), kind=kLoop, calls=%fused_computation.140 | loop fusion | bytes 1179648 | tf_op jit(solution)/shard_map/slice | solution.py:34
  3.4 1.3 %collective-permute-start = (f32[2,6,4,12,128]{4,2,3,1,0:T(4,128)}, f32[2,6,4,12,128]{4,2,3,1,0:T(4,128)}, u32[]{:S(2)}, u32[]{:S(2)}) collective-permute-start(f32[2,6,4,12,128]{4,2,3,1,0:T(4,128)} %get-tuple-element.11), channel_id=1, source_target_pairs={{16,0},{32,16},{48,32},{64,48},{80,64},{96,80},{112,96},{128,112},... | collective-permute-start | bytes 884744 | tf_op jit(solution)/shard_map/ppermute | solution.py:36
  4.7 6.8 %collective-permute-start.1 = (f32[2,6,4,12,128]{4,2,3,1,0:T(4,128)}, f32[2,6,4,12,128]{4,2,3,1,0:T(4,128)}, u32[]{:S(2)}, u32[]{:S(2)}) collective-permute-start(f32[2,6,4,12,128]{4,2,3,1,0:T(4,128)} %get-tuple-element.12), channel_id=1, source_target_pairs={{0,16},{16,32},{32,48},{48,64},{64,80},{80,96},{96,112},{112,128},... | collective-permute-start | bytes 884744 | tf_op jit(solution)/shard_map/ppermute | solution.py:35
  11.5 1.9 %copy.108 = f32[2,6,16,12,128]{4,0,3,1,2:T(2,128)} copy(f32[2,6,16,12,128]{4,2,3,1,0:T(8,128)S(1)} %pad_maximum_fusion.1) | data formatting | bytes 2359296 | tf_op jit(solution)/shard_map/concatenate | solution.py:81
  13.4 10.4 %all-to-all-start = ((f32[2,6,16,12,128]{4,0,3,1,2:T(2,128)}), f32[2,6,16,12,128]{4,0,3,1,2:T(2,128)S(1)}, u32[]{:S(2)}, u32[]{:S(2)}) async-start(f32[2,6,16,12,128]{4,0,3,1,2:T(2,128)} %copy.108), calls=%async_computation | async-start | bytes 2359296 | tf_op jit(solution)/shard_map/all_to_all | solution.py:194
  23.8 0.0 copy-done.21
  23.8 0.1 broadcast_multiply_fusion.6
  23.9 0.0 copy-done.8
  23.9 1.6 %broadcast_multiply_fusion.2 = (f32[16,12,128]{2,0,1:T(8,128)}, f32[16,12,128]{2,0,1:T(8,128)S(1)}, f32[16,12,128]{2,0,1:T(8,128)S(1)}) fusion(f32[16,12,128]{2,0,1:T(8,128)S(1)} %copy-done.8, f32[12]{0:T(128)S(1)} %get-tuple-element.30, f32[12]{0:T(128)S(1)} %get-tuple-element.32, f32[16,12,128]{2,0,1:T(8,128)} %param.12), kind=kLoop, calls=%fused_computation.132 | loop fusion | flops 73728 | bytes 491616 | tf_op jit(solution)/shard_map/mul | solution.py:156
  25.5 0.9 broadcast_multiply_fusion.5
  26.4 1.0 %slice_multiply_fusion.10 = (f32[1,1,16,12,128]{4,2,3,1,0:T(8,128)}, f32[1,1,16,12,128]{4,2,3,1,0:T(8,128)}, f32[1,1,16,12,128]{4,2,3,1,0:T(8,128)}, f32[1,1,16,...) fusion(f32[2,5,16,12,128]{4,2,3,1,0:T(8,128)S(1)} %copy-done), kind=kLoop, calls=%fused_computation.91 | loop fusion | flops 245760 | bytes 1966080 | tf_op jit(solution)/shard_map/mul | solution.py:116
  27.4 0.0 collective-permute-done
  27.4 0.0 collective-permute-done.1
  27.4 1.5 %pad_maximum_fusion = (f32[2,6,20,12,128]{4,2,3,1,0:T(8,128)S(1)}, f32[2,6,20,12,128]{4,2,3,1,0:T(8,128)S(1)}) fusion(f32[2,6,4,12,128]{4,2,3,1,0:T(4,128)} %collective-permute-done, f32[2,2,16,12,128]{4,2,3,1,0:T(8,128)S(1)} %slice.247, f32[2,1,16,12,128]{4,2,3,1,0:T(8,128)S(1)} %divide_subtract_fusion, f32[2,3,16,12,128]{4,2,3,1,0:T(8,128)S(1)} %slice.244, ...), kind=kLoop, calls=%fused_computation | loop fusion | flops 2211840 | bytes 4718592 | tf_op jit(solution)/shard_map/concatenate | solution.py:37
  28.8 0.0 copy-done.23
  28.9 3.0 %multiply_add_fusion = (f32[2,6,16,12,128]{4,2,3,1,0:T(8,128)S(1)}, f32[2,6,16,12,128]{4,2,3,1,0:T(8,128)S(1)}, f32[2,6,16,12,128]{4,2,3,1,0:T(8,128)}) fusion(f32[16,12,128]{2,0,1:T(8,128)S(1)} %get-tuple-element.29, f32[16,12,128]{2,0,1:T(8,128)S(1)} %get-tuple-element.34, f32[2,6,20,12,128]{4,2,3,1,0:T(8,128)S(1)} %get-tuple-element.10, ...), kind=kOutput, calls=%fused_computation.19 | convolution fusion | flops 457703424 | bytes 14417920 | tf_op jit(solution)/shard_map/dot_general | solution.py:104
  31.8 0.1 broadcast_multiply_fusion
  31.9 0.0 copy-start.3
  31.9 0.8 copy-done.22
  32.7 1.4 %fusion = f32[2,4,16,12,128]{4,2,3,1,0:T(8,128)S(1)} fusion(f32[128,128,1,1,1]{1,0,4,3,2:T(8,128)S(1)} %copy-done.22, f32[2,6,20,12,128]{4,2,3,1,0:T(8,128)S(1)} %get-tuple-element.10, f32[2,6,20,12,128]{4,2,3,1,0:T(8,128)S(1)} %get-tuple-element.9, f32[2,1,16,12,128]{4,2,3,1,0:T(8,128)S(1)} %divide_subtract_fusion, f32[2,3,16,12,128]{4,2,3,1,0:T(8,128)S(1)} %slice.244, ...), kind=kOutput, calls=%fused_computation.5 | convolution fusion | flops 305528832 | bytes 8716800 | tf_op jit(solution)/shard_map/dot_general | solution.py:105
  34.1 0.0 copy-start.6
  34.1 0.0 copy-done.5
  34.1 0.0 copy-done.3
  34.1 0.9 copy-done.6
  35.0 0.7 fusion.38
  35.8 5.3 %all-to-all-done = f32[2,6,16,12,128]{4,0,3,1,2:T(2,128)S(1)} async-done(((f32[2,6,16,12,128]{4,0,3,1,2:T(2,128)}), f32[2,6,16,12,128]{4,0,3,1,2:T(2,128)S(1)}, u32[]{:S(2)}, u32[]{:S(2)}) %all-to-all-start) | async-done | bytes 1179680 | tf_op jit(solution)/shard_map/all_to_all | solution.py:194
  41.0 0.1 copy.109
  41.1 0.8 copy-done.20
  41.9 1.2 %convolution_bitcast_fusion = f32[2,6,1,192,128]{4,3,1,0,2:T(8,128)S(1)} fusion(f32[192,192,1,1]{1,0,3,2:T(8,128)S(1)} %copy-done.20, f32[2,6,192,128]{3,0,2,1:T(2,128)S(1)} %bitcast.102), kind=kOutput, calls=%fused_computation.2 | convolution fusion | flops 679477248 | bytes 2506752 | tf_op jit(solution)/shard_map/sj,abxjt->abxst/dot_general | solution.py:110
  43.1 1.9 %copy.111 = f32[2,6,1,192,128]{4,0,2,1,3:T(2,128)} copy(f32[2,6,1,192,128]{4,3,1,0,2:T(8,128)S(1)} %convolution_bitcast_fusion) | data formatting | bytes 2359296 | tf_op jit(solution)/shard_map/sj,abxjt->abxst/transpose | solution.py:110
  45.1 4.5 %all-to-all-start.1 = ((f32[2,6,1,192,128]{4,0,2,1,3:T(2,128)}), f32[2,6,1,192,128]{4,0,2,1,3:T(2,128)S(1)}, u32[]{:S(2)}, u32[]{:S(2)}) async-start(f32[2,6,1,192,128]{4,0,2,1,3:T(2,128)} %copy.111), calls=%async_computation.1 | async-start | bytes 2359296 | tf_op jit(solution)/shard_map/all_to_all | solution.py:199
  49.5 0.1 slice.306
  49.6 0.9 copy-done.19
  50.4 0.9 convolution_bitcast_fusion.1
  51.6 1.2 %copy.116 = f32[16,2,4,1,12,128]{5,2,4,3,1,0:T(4,128)} copy(f32[16,2,4,1,12,128]{5,4,2,1,3,0:T(8,128)S(1)} %fusion.50) | data formatting | bytes 1572864 | tf_op jit(solution)/shard_map/stack | solution.py:19
  52.8 0.0 copy-start.17
  52.8 13.9 %all-to-all-done.1 = f32[2,6,1,192,128]{4,0,2,1,3:T(2,128)S(1)} async-done(((f32[2,6,1,192,128]{4,0,2,1,3:T(2,128)}), f32[2,6,1,192,128]{4,0,2,1,3:T(2,128)S(1)}, u32[]{:S(2)}, u32[]{:S(2)}) %all-to-all-start.1) | async-done | bytes 1179680 | tf_op jit(solution)/shard_map/all_to_all | solution.py:199
  66.7 5.0 %all-to-all-start.2 = ((f32[16,2,4,1,12,128]{5,2,4,3,1,0:T(4,128)}), f32[16,2,4,1,12,128]{5,2,4,3,1,0:T(4,128)}, u32[]{:S(2)}, u32[]{:S(2)}) async-start(f32[16,2,4,1,12,128]{5,2,4,3,1,0:T(4,128)} %copy.116), calls=%async_computation.2 | async-start | bytes 1572864 | tf_op jit(solution)/shard_map/all_to_all | solution.py:18
  71.7 0.0 copy-done.7
  71.7 2.0 %fusion.35 = f32[2,5,16,12,128]{4,2,3,1,0:T(8,128)} fusion(f32[2,5,16,12,128]{4,2,3,1,0:T(8,128)} %fusion.38, f32[2,4,16,12,128]{4,2,3,1,0:T(8,128)S(1)} %copy-done.7, f32[2,6,16,12,128]{4,2,3,1,0:T(8,128)} %copy-done.5, f32[1,1,16,12,128]{4,2,3,1,0:T(8,128)} %get-tuple-element.19, f32[1,1,16,12,128]{4,2,3,1,0:T(8,128)} %get-tuple-element.20, ...), kind=kLoop, calls=%fused_computation.63 | loop fusion | flops 491520 | bytes 1474608
  73.7 0.0 copy-done.9
  73.7 0.0 copy-done.10
  73.7 0.0 copy-done.16
  73.7 0.0 copy-done.17
  73.7 2.0 %fusion.29 = f32[2,5,16,12,128]{4,2,3,1,0:T(8,128)} fusion(f32[2,5,16,12,128]{4,2,3,1,0:T(8,128)} %fusion.35, f32[2,6,16,12,128]{4,2,3,1,0:T(8,128)} %get-tuple-element.33, f32[2,4,16,12,128]{4,2,3,1,0:T(8,128)S(1)} %copy-done.7, f32[2,6,16,12,128]{4,2,3,1,0:T(8,128)} %copy-done.5, f32[1,1,16,12,128]{4,2,3,1,0:T(8,128)S(1)} %copy-done.16, ...), kind=kLoop, calls=%fused_computation.54 | loop fusion | flops 786432 | bytes 1867872
  75.7 0.0 copy-done.11
  75.7 1.4 %broadcast_multiply_fusion.1 = (f32[2,6,16,12,128]{4,2,3,1,0:T(8,128)}, f32[2,6,16,12,128]{4,2,3,1,0:T(8,128)S(1)}) fusion(f32[16,12,128]{2,0,1:T(8,128)S(1)} %copy-done.11, f32[2,6,16,12,128]{4,0,1,3,2:T(2,128)S(1)} %bitcast.104), kind=kLoop, calls=%fused_computation.38 | loop fusion | flops 294912 | bytes 3637248 | tf_op jit(solution)/shard_map/mul | solution.py:121
  77.1 7.4 %all-to-all-done.2 = f32[16,2,4,1,12,128]{5,2,4,3,1,0:T(4,128)} async-done(((f32[16,2,4,1,12,128]{5,2,4,3,1,0:T(4,128)}), f32[16,2,4,1,12,128]{5,2,4,3,1,0:T(4,128)}, u32[]{:S(2)}, u32[]{:S(2)}) %all-to-all-start.2) | async-done | bytes 786464 | tf_op jit(solution)/shard_map/all_to_all | solution.py:18
  84.5 1.8 %fusion.18 = f32[2,4,16,12,128]{4,2,3,1,0:T(8,128)S(1)} fusion(f32[2,6,16,12,128]{4,2,3,1,0:T(8,128)S(1)} %get-tuple-element.14, f32[16,2,4,1,12,128]{5,2,4,3,1,0:T(4,128)} %all-to-all-done.2, f32[12]{0:T(128)S(1)} %get-tuple-element.32), kind=kLoop, calls=%fused_computation.34 | loop fusion | flops 393216 | bytes 2359344 | tf_op jit(solution)/shard_map/add | solution.py:120
  86.2 0.0 copy-done.2
  86.3 0.0 copy-done.4
  86.3 0.0 copy-done.14
  86.3 1.2 %fusion.23 = (f32[2,5,16,12,128]{4,2,3,1,0:T(8,128)S(1)}, f32[2,1,16,12,128]{4,2,3,1,0:T(8,128)S(1)}, f32[2,5,16,12,128]{4,2,3,1,0:T(8,128)S(1)}) fusion(f32[2,5,16,12,128]{4,2,3,1,0:T(8,128)S(1)} %copy-done.4, f32[2,6,16,12,128]{4,2,3,1,0:T(8,128)} %copy-done.5, f32[1,1,16,12,128]{4,2,3,1,0:T(8,128)S(1)} %copy-done.15, ...), kind=kLoop, calls=%fused_computation.47 | loop fusion | flops 540672 | bytes 2261504
  87.6 0.8 copy-done.12
  88.4 0.0 copy-done.13
  88.5 1.1 %fusion.20 = (f32[2,5,16,12,128]{4,2,3,1,0:T(8,128)S(1)}, f32[2,5,16,12,128]{4,2,3,1,0:T(8,128)S(1)}) fusion(f32[2,5,16,12,128]{4,2,3,1,0:T(8,128)S(1)} %get-tuple-element.5, f32[2,4,16,12,128]{4,2,3,1,0:T(8,128)} %copy-done.6, f32[2,6,16,12,128]{4,2,3,1,0:T(8,128)} %copy-done.5, f32[1,1,16,12,128]{4,2,3,1,0:T(8,128)S(1)} %copy-done.13, ...), kind=kLoop, calls=%fused_computation.41 | loop fusion | flops 491520 | bytes 1867776 | tf_op jit(solution)/shard_map/stack | solution.py:173
  89.6 1.1 %add.150 = f32[2,5,16,12,128]{4,2,3,1,0:T(8,128)} add(f32[2,5,16,12,128]{4,2,3,1,0:T(8,128)S(1)} %get-tuple-element.26, f32[2,5,16,12,128]{4,2,3,1,0:T(8,128)S(1)} %get-tuple-element.25) | non-fusion elementwise | flops 245760 | bytes 2949120 | tf_op jit(solution)/shard_map/add | solution.py:203
  (42 shorter events, 0.3 us)
Async XLA Ops:
  0.0 2.3 %copy-start = (f32[2,5,16,12,128]{4,2,3,1,0:T(8,128)S(1)}, f32[2,5,16,12,128]{4,2,3,1,0:T(8,128)}, u32[]{:S(2)}) copy-start(f32[2,5,16,12,128]{4,2,3,1,0:T(8,128)} %param.11) | copy-start | bytes 2949124
  0.0 2.3 %copy-start.1 = (f32[16,12,128]{2,0,1:T(8,128)S(1)}, f32[16,12,128]{2,0,1:T(8,128)}, u32[]{:S(2)}) copy-start(f32[16,12,128]{2,0,1:T(8,128)} %param.15) | copy-start | bytes 294916
  0.0 2.3 %copy-start.18 = (f32[16,12,128]{2,0,1:T(8,128)S(1)}, f32[16,12,128]{2,0,1:T(8,128)}, u32[]{:S(2)}) copy-start(f32[16,12,128]{2,0,1:T(8,128)} %param.16) | copy-start | bytes 294916
  3.4 24.0 %collective-permute-start = (f32[2,6,4,12,128]{4,2,3,1,0:T(4,128)}, f32[2,6,4,12,128]{4,2,3,1,0:T(4,128)}, u32[]{:S(2)}, u32[]{:S(2)}) collective-permute-start(f32[2,6,4,12,128]{4,2,3,1,0:T(4,128)} %get-tuple-element.11), channel_id=1, source_target_pairs={{16,0},{32,16},{48,32},{64,48},{80,64},{96,80},{112,96},{128,112},... | collective-permute-start | bytes 884744 | tf_op jit(solution)/shard_map/ppermute | solution.py:36
  4.7 22.7 %collective-permute-start.1 = (f32[2,6,4,12,128]{4,2,3,1,0:T(4,128)}, f32[2,6,4,12,128]{4,2,3,1,0:T(4,128)}, u32[]{:S(2)}, u32[]{:S(2)}) collective-permute-start(f32[2,6,4,12,128]{4,2,3,1,0:T(4,128)} %get-tuple-element.12), channel_id=1, source_target_pairs={{0,16},{16,32},{32,48},{48,64},{64,80},{80,96},{96,112},{112,128},... | collective-permute-start | bytes 884744 | tf_op jit(solution)/shard_map/ppermute | solution.py:35
  13.4 10.4 %copy-start.21 = (f32[192]{0:T(256)S(1)}, f32[192]{0:T(256)}, u32[]{:S(2)}) copy-start(f32[192]{0:T(256)} %constant.58.clone) | copy-start | bytes 2308
  13.4 10.5 %copy-start.8 = (f32[16,12,128]{2,0,1:T(8,128)S(1)}, f32[16,12,128]{2,0,1:T(8,128)}, u32[]{:S(2)}) copy-start(f32[16,12,128]{2,0,1:T(8,128)} %param.14) | copy-start | bytes 294916
  13.4 27.6 %all-to-all-start = ((f32[2,6,16,12,128]{4,0,3,1,2:T(2,128)}), f32[2,6,16,12,128]{4,0,3,1,2:T(2,128)S(1)}, u32[]{:S(2)}, u32[]{:S(2)}) async-start(f32[2,6,16,12,128]{4,0,3,1,2:T(2,128)} %copy.108), calls=%async_computation | async-start | bytes 2359296 | tf_op jit(solution)/shard_map/all_to_all | solution.py:194
  27.4 1.5 %copy-start.23 = (f32[128,128,1,1,1]{1,0,4,3,2:T(8,128)S(1)}, f32[128,128,1,1,1]{1,0,4,3,2:T(8,128)}, u32[]{:S(2)}) copy-start(f32[128,128,1,1,1]{1,0,4,3,2:T(8,128)} %constant.69) | copy-start | bytes 196612
  31.8 2.3 %copy-start.5 = (f32[2,6,16,12,128]{4,2,3,1,0:T(8,128)}, f32[2,6,16,12,128]{4,2,3,1,0:T(8,128)S(1)}, u32[]{:S(2)}) copy-start(f32[2,6,16,12,128]{4,2,3,1,0:T(8,128)S(1)} %get-tuple-element.7) | copy-start | bytes 3538948
  31.8 0.9 copy-start.22
  31.9 2.2 %copy-start.3 = (f32[2,6,16,12,128]{4,2,3,1,0:T(8,128)}, f32[2,6,16,12,128]{4,2,3,1,0:T(8,128)S(1)}, u32[]{:S(2)}) copy-start(f32[2,6,16,12,128]{4,2,3,1,0:T(8,128)S(1)} %broadcast_multiply_fusion) | copy-start | bytes 3538948
  34.1 0.9 %copy-start.6 = (f32[2,4,16,12,128]{4,2,3,1,0:T(8,128)}, f32[2,4,16,12,128]{4,2,3,1,0:T(8,128)S(1)}, u32[]{:S(2)}) copy-start(f32[2,4,16,12,128]{4,2,3,1,0:T(8,128)S(1)} %fusion) | copy-start | bytes 2359300
  41.0 0.9 %copy-start.20 = (f32[192,192,1,1]{1,0,3,2:T(8,128)S(1)}, f32[192,192,1,1]{1,0,3,2:T(8,128)}, u32[]{:S(2)}) copy-start(f32[192,192,1,1]{1,0,3,2:T(8,128)} %constant.67) | copy-start | bytes 442372
  45.1 21.7 %all-to-all-start.1 = ((f32[2,6,1,192,128]{4,0,2,1,3:T(2,128)}), f32[2,6,1,192,128]{4,0,2,1,3:T(2,128)S(1)}, u32[]{:S(2)}, u32[]{:S(2)}) async-start(f32[2,6,1,192,128]{4,0,2,1,3:T(2,128)} %copy.111), calls=%async_computation.1 | async-start | bytes 2359296 | tf_op jit(solution)/shard_map/all_to_all | solution.py:199
  49.5 0.9 %copy-start.19 = (f32[192,192,1,1]{1,0,3,2:T(8,128)S(1)}, f32[192,192,1,1]{1,0,3,2:T(8,128)}, u32[]{:S(2)}) copy-start(f32[192,192,1,1]{1,0,3,2:T(8,128)} %constant.68) | copy-start | bytes 442372
  52.8 18.9 %copy-start.7 = (f32[2,4,16,12,128]{4,2,3,1,0:T(8,128)S(1)}, f32[2,4,16,12,128]{4,2,3,1,0:T(8,128)}, u32[]{:S(2)}) copy-start(f32[2,4,16,12,128]{4,2,3,1,0:T(8,128)} %copy-done.6) | copy-start | bytes 2359300
  52.8 20.9 %copy-start.9 = (f32[16,12,128]{2,0,1:T(8,128)S(1)}, f32[16,12,128]{2,0,1:T(8,128)}, u32[]{:S(2)}) copy-start(f32[16,12,128]{2,0,1:T(8,128)} %param.14) | copy-start | bytes 294916
  52.8 20.9 %copy-start.10 = (f32[16,12,128]{2,0,1:T(8,128)S(1)}, f32[16,12,128]{2,0,1:T(8,128)}, u32[]{:S(2)}) copy-start(f32[16,12,128]{2,0,1:T(8,128)} %param.13) | copy-start | bytes 294916
  52.8 20.9 %copy-start.16 = (f32[1,1,16,12,128]{4,2,3,1,0:T(8,128)S(1)}, f32[1,1,16,12,128]{4,2,3,1,0:T(8,128)}, u32[]{:S(2)}) copy-start(f32[1,1,16,12,128]{4,2,3,1,0:T(8,128)} %get-tuple-element.17) | copy-start | bytes 294916
  52.8 20.9 %copy-start.17 = (f32[1,1,16,12,128]{4,2,3,1,0:T(8,128)S(1)}, f32[1,1,16,12,128]{4,2,3,1,0:T(8,128)}, u32[]{:S(2)}) copy-start(f32[1,1,16,12,128]{4,2,3,1,0:T(8,128)} %get-tuple-element.18) | copy-start | bytes 294916
  66.7 17.7 %all-to-all-start.2 = ((f32[16,2,4,1,12,128]{5,2,4,3,1,0:T(4,128)}), f32[16,2,4,1,12,128]{5,2,4,3,1,0:T(4,128)}, u32[]{:S(2)}, u32[]{:S(2)}) async-start(f32[16,2,4,1,12,128]{5,2,4,3,1,0:T(4,128)} %copy.116), calls=%async_computation.2 | async-start | bytes 1572864 | tf_op jit(solution)/shard_map/all_to_all | solution.py:18
  73.7 2.0 %copy-start.11 = (f32[16,12,128]{2,0,1:T(8,128)S(1)}, f32[16,12,128]{2,0,1:T(8,128)}, u32[]{:S(2)}) copy-start(f32[16,12,128]{2,0,1:T(8,128)} %param.13) | copy-start | bytes 294916
  84.5 1.8 %copy-start.2 = (f32[2,6,16,12,128]{4,2,3,1,0:T(8,128)S(1)}, f32[2,6,16,12,128]{4,2,3,1,0:T(8,128)}, u32[]{:S(2)}) copy-start(f32[2,6,16,12,128]{4,2,3,1,0:T(8,128)} %get-tuple-element.13) | copy-start | bytes 3538948
  84.5 1.8 %copy-start.4 = (f32[2,5,16,12,128]{4,2,3,1,0:T(8,128)S(1)}, f32[2,5,16,12,128]{4,2,3,1,0:T(8,128)}, u32[]{:S(2)}) copy-start(f32[2,5,16,12,128]{4,2,3,1,0:T(8,128)} %fusion.29) | copy-start | bytes 2949124
  84.5 1.8 %copy-start.14 = (f32[1,1,16,12,128]{4,2,3,1,0:T(8,128)S(1)}, f32[1,1,16,12,128]{4,2,3,1,0:T(8,128)}, u32[]{:S(2)}) copy-start(f32[1,1,16,12,128]{4,2,3,1,0:T(8,128)} %get-tuple-element.16) | copy-start | bytes 294916
  84.5 1.8 %copy-start.15 = (f32[1,1,16,12,128]{4,2,3,1,0:T(8,128)S(1)}, f32[1,1,16,12,128]{4,2,3,1,0:T(8,128)}, u32[]{:S(2)}) copy-start(f32[1,1,16,12,128]{4,2,3,1,0:T(8,128)} %get-tuple-element.23) | copy-start | bytes 294916
  87.5 0.9 copy-start.12
  87.6 0.9 %copy-start.13 = (f32[1,1,16,12,128]{4,2,3,1,0:T(8,128)S(1)}, f32[1,1,16,12,128]{4,2,3,1,0:T(8,128)}, u32[]{:S(2)}) copy-start(f32[1,1,16,12,128]{4,2,3,1,0:T(8,128)} %get-tuple-element.24) | copy-start | bytes 294916
